TPU v7x, 32 devices: a whole 2x2x4 slice. The times are simulated.
32 devices in a mesh: dp: 2 (over x), expert: 4 (over y, core), tensor: 4 (over z).
Axes of the slice: x: 2, y: 2, z: 4, core: 2. Of those that a mesh axis runs over, the one named last changes fastest.
Arguments:
- output_grad: bfloat16 [2048, 4096], P(('dp', 'expert'), 'tensor'), may hold values from -6 to 6
- expert_ids: int32 [2048, 2], P(('dp', 'expert')), may hold values from 0 to 3, all different within a row; in each aligned block of 256 rows (0 to 255, 256 to 511, ...) at most 192 rows name the same one
- router_weights: bfloat16 [2048, 2], P(('dp', 'expert')), may hold values from 0.099609375 to 0.8984375
- gate_preact: bfloat16 [4, 1536, 14336], P('expert', 'dp', 'tensor'), may hold values from -6 to 6
- up_preact: bfloat16 [4, 1536, 14336], P('expert', 'dp', 'tensor'), may hold values from -6 to 6
- down_weight: bfloat16 [4, 14336, 4096], P('expert', 'tensor', 'dp'), may hold values from -0.046875 to 0.046875
Outputs:
- gate_preact_grad: bfloat16 [4, 1536, 14336], P('expert', 'dp', 'tensor')
- up_preact_grad: bfloat16 [4, 1536, 14336], P('expert', 'dp', 'tensor')
- down_grad: bfloat16 [4, 14336, 4096], P('expert', 'tensor', 'dp')
- router_grad: float32 [2048, 2], P(('dp', 'expert'))
Inputs may be any that keep to these rules, and one draw needn't show every extreme that they name: `expert_ids`: the ids of one token differ. Among the 256 rows of one device no expert is named by more than 192 rows, and in every draw some expert is named by exactly 192 rows of some device.
All inputs are finite; a program needn't handle non-finite values.
Results may differ from a plain program's by a relative error of at most 0.007.
Values may be sent and summed in bfloat16 or wider, within the bound.
No kernel may reach another device: no remote copies, remote signals or barrier semaphores. Data moves between devices by JAX's collectives and lax.ppermute only.
A program may use at most 192 MiB of HBM per device.

v0:
```python
import jax
import jax.numpy as jnp
from jax import lax
from jax.sharding import PartitionSpec as P

PARTIAL_DTYPE = jnp.float32


def silu_parts(values):
    sigma = jax.nn.sigmoid(values)
    return (values * sigma, sigma * (1.0 + values * (1.0 - sigma)))


def swap_dp(value):
    return lax.ppermute(value, "dp", perm=[(0, 1), (1, 0)])


def local(output_grad, expert_ids, router_weights, gate_preact, up_preact, down_weight):
    expert_count = lax.axis_size("expert")
    tensor_count = lax.axis_size("tensor")
    replica = lax.axis_index("dp")
    part = lax.axis_index("tensor")
    tokens_here = expert_ids.shape[0]
    choices_each = expert_ids.shape[1]
    capacity = gate_preact.shape[1] // expert_count
    flat_ids = expert_ids.reshape(-1)
    one_hot = (flat_ids[:, None] == jnp.arange(expert_count, dtype=jnp.int32)).astype(jnp.int32)
    earlier = jnp.cumsum(one_hot, axis=0) - one_hot
    slot_index = jnp.sum(earlier * one_hot, axis=1)
    target = (flat_ids * capacity + slot_index).reshape(tokens_here, choices_each)
    columns = jnp.arange(expert_count * capacity, dtype=jnp.int32)
    matches = [target[:, which][:, None] == columns[None, :] for which in range(choices_each)]
    selector = jnp.zeros((tokens_here, expert_count * capacity), jnp.bfloat16)
    gate_table = jnp.zeros((tokens_here, expert_count * capacity), jnp.float32)
    for which in range(choices_each):
        selector = jnp.where(matches[which], jnp.bfloat16(1.0), selector)
        gate_table = jnp.where(
            matches[which], router_weights[:, which : which + 1].astype(jnp.float32), gate_table
        )
    gate_send = jnp.sum(gate_table, axis=0).astype(jnp.bfloat16).reshape(expert_count, capacity)
    gate_float = gate_preact[0].astype(jnp.float32)
    up_float = up_preact[0].astype(jnp.float32)
    active, slope = silu_parts(gate_float)
    hidden = (active * up_float).astype(jnp.bfloat16)
    contract_rows = (((0,), (0,)), ((), ()))
    contract_cols = (((1,), (1,)), ((), ()))
    outgoing = lax.dot_general(
        selector, output_grad, contract_rows, preferred_element_type=jnp.float32
    )
    outgoing = outgoing.astype(jnp.bfloat16).reshape(expert_count, capacity, -1)
    hidden, outgoing = lax.optimization_barrier((hidden, outgoing))
    hidden_other = swap_dp(hidden)
    received = lax.all_to_all(outgoing, "expert", split_axis=0, concat_axis=0, tiled=True)
    gate_slots = lax.all_to_all(gate_send, "expert", split_axis=0, concat_axis=0, tiled=True)
    slots = expert_count * capacity
    narrow_rows = received.reshape(slots, -1)
    gate_bf16 = gate_slots.reshape(-1)
    gate_column = gate_bf16.astype(jnp.float32)[:, None]
    fragment = lax.all_gather(narrow_rows, "tensor", axis=1, tiled=True)
    width = fragment.shape[1]
    half = width // 2
    piece = half // tensor_count
    own_rows = lax.dynamic_slice_in_dim(fragment, replica * half, half, axis=1)
    send_rows = lax.dynamic_slice_in_dim(
        fragment, (1 - replica) * half + part * piece, piece, axis=1
    )
    other_piece = swap_dp(send_rows)
    other_rows = lax.all_gather(other_piece, "tensor", axis=1, tiled=True)
    hidden_other, other_rows = lax.optimization_barrier((hidden_other, other_rows))
    other_gates = swap_dp(gate_bf16).astype(jnp.float32)[:, None]
    local_weight = down_weight[0]
    partial_other = lax.dot_general(
        other_rows, local_weight, contract_cols, preferred_element_type=jnp.float32
    )
    partial_back = swap_dp(partial_other.astype(PARTIAL_DTYPE)).astype(jnp.float32)
    partial_own = lax.dot_general(
        own_rows, local_weight, contract_cols, preferred_element_type=jnp.float32
    )
    scaled_own = (gate_column * own_rows.astype(jnp.float32)).astype(jnp.bfloat16)
    scaled_other = (other_gates * other_rows.astype(jnp.float32)).astype(jnp.bfloat16)
    grad_own = lax.dot_general(
        hidden, scaled_own, contract_rows, preferred_element_type=jnp.float32
    )
    grad_other = lax.dot_general(
        hidden_other, scaled_other, contract_rows, preferred_element_type=jnp.float32
    )
    rounded_own = lax.optimization_barrier(grad_own.astype(jnp.bfloat16))
    rounded_other = lax.optimization_barrier(grad_other.astype(jnp.bfloat16))
    partial_back, rounded_own, rounded_other = lax.optimization_barrier(
        (partial_back, rounded_own, rounded_other)
    )
    upstream = partial_own + partial_back
    down_grad = (rounded_own.astype(jnp.float32) + rounded_other.astype(jnp.float32)).astype(
        jnp.bfloat16
    )
    score = jnp.sum(hidden.astype(jnp.float32) * upstream, axis=1)
    hidden_grad = gate_column * upstream
    gate_grad = (hidden_grad * up_float * slope).astype(jnp.bfloat16)
    up_grad = (hidden_grad * active).astype(jnp.bfloat16)
    summed_scores = lax.psum(score, "tensor")
    returned = lax.all_to_all(
        summed_scores.reshape(expert_count, capacity),
        "expert",
        split_axis=0,
        concat_axis=0,
        tiled=True,
    )
    flat_scores = returned.reshape(-1)
    router_grad = jnp.stack(
        [
            jnp.sum(jnp.where(matches[which], flat_scores[None, :], 0.0), axis=1)
            for which in range(choices_each)
        ],
        axis=1,
    )
    return (gate_grad[None], up_grad[None], down_grad[None], router_grad)


def solution(mesh):
    placed = (
        P(("dp", "expert"), "tensor"),
        P(("dp", "expert"), None),
        P(("dp", "expert"), None),
        P("expert", "dp", "tensor"),
        P("expert", "dp", "tensor"),
        P("expert", "tensor", "dp"),
    )
    return jax.shard_map(
        local,
        mesh=mesh,
        in_specs=placed,
        out_specs=(
            P("expert", "dp", "tensor"),
            P("expert", "dp", "tensor"),
            P("expert", "tensor", "dp"),
            P(("dp", "expert"), None),
        ),
        check_vma=False,
    )
```

profile of v0, /device:TPU:1, one launch (start us, length us, event | category | flops | bytes accessed | tf_op | source)
XLA Modules:
  0.0 616.6 jit_solution(12437453717802722302)
XLA Ops:
  7.2 0.0 copy-start
  7.2 0.0 all-gather.3.cloned.1.call-start
  7.2 0.9 copy.28
  8.1 0.1 eq.59
  8.2 0.1 eq.55
  8.4 1.2 reduce-window.6
  9.6 0.2 slice_reduce_fusion
  9.8 0.2 reduce-window.9
  10.0 0.1 add_bitcast_fusion
  10.1 0.1 reduce_sum.48
  10.3 0.1 copy.30
  10.3 0.7 multiply_add_fusion
  11.1 8.8 %fusion.5 = bf16[768,3584]{1,0:T(8,128)(2,1)} fusion(bf16[1,768,3584]{2,1,0:T(8,128)(2,1)} %param.10, bf16[1,768,3584]{2,1,0:T(8,128)(2,1)} %param.9), kind=kLoop, calls=%fused_computation.13 | loop fusion | flops 22020096 | bytes 16515072 | tf_op jit(solution)/shard_map/convert_element_type | solution.py:44
  19.9 0.8 convolution_convert_fusion.2
  20.7 23.2 %all_to_all.20 = bf16[4,192,1024]{2,1,0:T(8,128)(2,1)} all-to-all(bf16[4,192,1024]{2,1,0:T(8,128)(2,1)S(1)} %bitcast.61), channel_id=1, replica_groups=mesh['dp'=2,'expert'=4,'tensor'=4] {'expert'}, dimensions={0} | all-to-all | bytes 3145728 | tf_op jit(solution)/shard_map/all_to_all | solution.py:53
  43.9 0.0 all-gather.3.cloned.1.call-update
  43.9 0.0 all-gather.5.cloned.1.call-start
  44.0 1.8 collective-permute-start
  45.7 115.1 %all-gather.3.cloned.1.call-done = bf16[768,4096]{1,0:T(8,128)(2,1)} async-done(((bf16[768,1024]{1,0:T(8,128)(2,1)}), bf16[768,4096]{1,0:T(8,128)(2,1)}) %all-gather.3.cloned.1.call-update) | async-done | bytes 6291472 | tf_op jit(solution)/shard_map/all_gather | solution.py:59
  160.8 1.2 constant_dynamic-slice_fusion
  162.0 1.2 collective-permute-start.1
  163.2 18.3 %collective-permute-done.1 = bf16[768,512]{1,0:T(8,128)(2,1)S(1)} collective-permute-done((bf16[768,512]{1,0:T(8,128)(2,1)S(1)}, bf16[768,512]{1,0:T(8,128)(2,1)S(1)}, u32[]{:S(2)}, u32[]{:S(2)}) %collective-permute-start.1) | collective-permute-done | bytes 786464 | tf_op jit(solution)/shard_map/ppermute | solution.py:15
  181.5 0.9 copy-done.2
  182.4 0.0 all-gather.5.cloned.1.call-update
  182.4 0.0 copy-start.3
  182.5 0.0 collective-permute-done
  182.5 64.6 %all-gather.5.cloned.1.call-done = bf16[768,2048]{1,0:T(8,128)(2,1)} async-done(((bf16[768,512]{1,0:T(8,128)(2,1)}), bf16[768,2048]{1,0:T(8,128)(2,1)}) %all-gather.5.cloned.1.call-update) | async-done | bytes 3145744 | tf_op jit(solution)/shard_map/all_gather | solution.py:68
  247.0 18.2 %fusion.1 = f32[768,3584]{1,0:T(8,128)} fusion(bf16[768,2048]{1,0:T(8,128)(2,1)} %all-gather.5.cloned.1.call-done, bf16[1,3584,2048]{2,1,0:T(8,128)(2,1)} %param.11), kind=kOutput, calls=%fused_computation.7 | convolution fusion | flops 11274289152 | bytes 28835840 | tf_op jit(solution)/shard_map/dot_general | solution.py:72
  265.2 1.2 collective-permute-start.2
  266.4 0.2 select_reduce_fusion.2
  266.6 0.1 convert_element_type.113
  266.7 7.0 %all_to_all.21 = bf16[4,1,192]{2,1,0:T(2,128)(2,1)S(1)} all-to-all(bf16[4,1,192]{2,1,0:T(2,128)(2,1)S(1)} %convert_element_type.113), channel_id=1, replica_groups=mesh['dp'=2,'expert'=4,'tensor'=4] {'expert'}, dimensions={0} | all-to-all | bytes 3072 | tf_op jit(solution)/shard_map/all_to_all | solution.py:54
  273.7 0.1 reshape.71
  273.8 0.3 collective-permute-start.3
  274.1 229.0 %collective-permute-done.3 = bf16[768]{0:T(1024)(128)(2,1)S(1)} collective-permute-done((bf16[768]{0:T(1024)(128)(2,1)S(1)}, bf16[768]{0:T(1024)(128)(2,1)S(1)}, u32[]{:S(2)}, u32[]{:S(2)}) %collective-permute-start.3) | collective-permute-done | bytes 1568 | tf_op jit(solution)/shard_map/ppermute | solution.py:15
  503.1 18.3 %convolution_convert_fusion.1 = bf16[3584,2048]{1,0:T(8,128)(2,1)} fusion(bf16[768,3584]{1,0:T(8,128)(2,1)} %fusion.5, f32[768]{0:T(1024)S(1)} %convert_element_type.91, bf16[768,4096]{1,0:T(8,128)(2,1)} %all-gather.3.cloned.1.call-done, s32[]{:T(128)S(6)} %select_n.31), kind=kOutput, calls=%fused_computation.5 | convolution fusion | flops 11286347776 | bytes 23333892 | tf_op jit(solution)/shard_map/dot_general | solution.py:81
  521.3 18.3 %fusion.3 = f32[768,3584]{1,0:T(8,128)} fusion(bf16[1,3584,2048]{2,1,0:T(8,128)(2,1)} %param.11, bf16[768,4096]{1,0:T(8,128)(2,1)} %all-gather.3.cloned.1.call-done, s32[]{:T(128)S(6)} %select_n.31), kind=kOutput, calls=%fused_computation.9 | convolution fusion | flops 11274289152 | bytes 28835844 | tf_op jit(solution)/shard_map/dot_general | solution.py:76
  539.6 17.9 %convolution_convert_fusion = bf16[3584,2048]{1,0:T(8,128)(2,1)} fusion(bf16[768,3584]{1,0:T(8,128)(2,1)} %collective-permute-done, bf16[768,2048]{1,0:T(8,128)(2,1)} %all-gather.5.cloned.1.call-done, f32[768]{0:T(1024)S(1)} %convert_element_type.101), kind=kOutput, calls=%fused_computation.4 | convolution fusion | flops 11286347776 | bytes 23333888 | tf_op jit(solution)/shard_map/dot_general | solution.py:84
  557.5 0.0 collective-permute-done.2
  557.5 17.8 %fusion.13 = (bf16[1,768,3584]{2,1,0:T(8,128)(2,1)}, bf16[1,768,3584]{2,1,0:T(8,128)(2,1)}, f32[768]{0:T(1024)S(1)}) fusion(f32[768]{0:T(1024)S(1)} %convert_element_type.91, bf16[1,768,3584]{2,1,0:T(8,128)(2,1)S(1)} %bitcast.59, f32[768,3584]{1,0:T(8,128)} %fusion.3, f32[768,3584]{1,0:T(8,128)} %collective-permute-done.2, bf16[1,768,3584]{2,1,0:T(8,128)(2,1)} %param.10, ...), kind=kLoop, calls=%fused_computation.25 | loop fusion | flops 55049472 | bytes 49551360 | tf_op jit(solution)/shard_map/broadcast_in_dim | solution.py:116
  575.4 0.1 all_to_all.15
  575.4 8.4 %psum.7 = f32[4,1,192]{2,1,0:T(1,128)} all-reduce(f32[4,1,192]{2,1,0:T(1,128)S(1)} %all_to_all.15), channel_id=1, replica_groups=mesh['dp'=2,'expert'=4,'tensor'=4] {'tensor'}, use_global_device_ids=true, to_apply=%region_5.6 | all-reduce | flops 768 | bytes 6144 | tf_op jit(solution)/shard_map/psum | solution.py:100
  583.9 6.2 %all-to-all-start.2 = ((f32[4,1,192]{2,1,0:T(1,128)}), f32[4,1,192]{2,1,0:T(1,128)S(1)}, u32[]{:S(2)}, u32[]{:S(2)}) async-start(f32[4,1,192]{2,1,0:T(1,128)} %psum.7), calls=%async_computation.2 | async-start | bytes 8192 | tf_op jit(solution)/shard_map/all_to_all | solution.py:101
  590.1 18.7 %fusion = bf16[1,3584,2048]{2,1,0:T(8,128)(2,1)} fusion(bf16[3584,2048]{1,0:T(8,128)(2,1)} %convolution_convert_fusion, bf16[3584,2048]{1,0:T(8,128)(2,1)} %convolution_convert_fusion.1), kind=kLoop, calls=%fused_computation.6 | loop fusion | flops 29360128 | bytes 44040192 | tf_op jit(solution)/shard_map/broadcast_in_dim | solution.py:116
  608.7 0.0 all-to-all-done.2
  608.8 0.1 broadcast_in_dim.76
  608.8 0.3 select_reduce_fusion.1
  609.2 0.6 pad_maximum_fusion
  (18 shorter events, 0.1 us)
Async XLA Ops:
  7.2 12.7 %copy-start = (bf16[256,1024]{1,0:T(8,128)(2,1)S(1)}, bf16[256,1024]{1,0:T(8,128)(2,1)}, u32[]{:S(2)}) copy-start(bf16[256,1024]{1,0:T(8,128)(2,1)} %param.6) | copy-start | bytes 1572868
  7.2 153.6 %all-gather.3.cloned.1.call-start = ((), (), s32[]{:S(2)}) async-start(), calls=%async_computation.3 | async-start | bytes 7864320 | tf_op jit(solution)/shard_map/all_gather | solution.py:59
  43.9 203.1 %all-gather.5.cloned.1.call-start = ((), (), s32[]{:S(2)}) async-start(), calls=%async_computation.4 | async-start | bytes 3932160 | tf_op jit(solution)/shard_map/all_gather | solution.py:68
  44.0 138.5 %collective-permute-start = (bf16[768,3584]{1,0:T(8,128)(2,1)}, bf16[768,3584]{1,0:T(8,128)(2,1)}, u32[]{:S(2)}, u32[]{:S(2)}) collective-permute-start(bf16[768,3584]{1,0:T(8,128)(2,1)} %fusion.5), channel_id=1, source_target_pairs={{0,16},{16,0},{1,17},{17,1},{2,18},{18,2},{3,19},{19,3},{4,20},{20... | collective-permute-start | bytes 16515080 | tf_op jit(solution)/shard_map/ppermute | solution.py:15
  162.0 19.6 %collective-permute-start.1 = (bf16[768,512]{1,0:T(8,128)(2,1)S(1)}, bf16[768,512]{1,0:T(8,128)(2,1)S(1)}, u32[]{:S(2)}, u32[]{:S(2)}) collective-permute-start(bf16[768,512]{1,0:T(8,128)(2,1)S(1)} %constant_dynamic-slice_fusion), channel_id=1, source_target_pairs={{0,16},{16,0},{1,17},{17,1},{2,18},{18,2},{3,19},{19,3},{4,20},{20... | collective-permute-start | bytes 2359304 | tf_op jit(solution)/shard_map/ppermute | solution.py:15
  181.5 0.9 copy-start.2
  182.4 83.9 %copy-start.3 = (bf16[256,2]{0,1:T(2,128)(2,1)S(1)}, bf16[256,2]{0,1:T(2,128)(2,1)}, u32[]{:S(2)}) copy-start(bf16[256,2]{0,1:T(2,128)(2,1)} %param.8) | copy-start | bytes 3076
  265.2 292.3 %collective-permute-start.2 = (f32[768,3584]{1,0:T(8,128)}, f32[768,3584]{1,0:T(8,128)}, u32[]{:S(2)}, u32[]{:S(2)}) collective-permute-start(f32[768,3584]{1,0:T(8,128)} %fusion.1), channel_id=1, source_target_pairs={{0,16},{16,0},{1,17},{17,1},{2,18},{18,2},{3,19},{19,3},{4,20},{20... | collective-permute-start | bytes 33030152 | tf_op jit(solution)/shard_map/ppermute | solution.py:15
  273.8 229.3 %collective-permute-start.3 = (bf16[768]{0:T(1024)(128)(2,1)S(1)}, bf16[768]{0:T(1024)(128)(2,1)S(1)}, u32[]{:S(2)}, u32[]{:S(2)}) collective-permute-start(bf16[768]{0:T(1024)(128)(2,1)S(1)} %reshape.71), channel_id=1, source_target_pairs={{0,16},{16,0},{1,17},{17,1},{2,18},{18,2},{3,19},{19,3},{4,20},{20... | collective-permute-start | bytes 4616 | tf_op jit(solution)/shard_map/ppermute | solution.py:15
  503.1 54.5 %slice-start = ((s8[5505024]{0:T(1024)(128)(4,1)}), s8[4194304]{0:T(1024)(128)(4,1)S(1)}, s32[]{:S(2)}) async-start(s8[5505024]{0:T(1024)(128)(4,1)} %bitcast.58), calls=%async_computation.5 | async-start | bytes 8388608
  521.3 36.2 %slice-start.1 = ((s8[5505024]{0:T(1024)(128)(4,1)}), s8[1310720]{0:T(1024)(128)(4,1)S(1)}, s32[]{:S(2)}) async-start(s8[5505024]{0:T(1024)(128)(4,1)} %bitcast.58), calls=%async_computation.6 | async-start | bytes 2621440
  583.9 24.9 %all-to-all-start.2 = ((f32[4,1,192]{2,1,0:T(1,128)}), f32[4,1,192]{2,1,0:T(1,128)S(1)}, u32[]{:S(2)}, u32[]{:S(2)}) async-start(f32[4,1,192]{2,1,0:T(1,128)} %psum.7), calls=%async_computation.2 | async-start | bytes 8192 | tf_op jit(solution)/shard_map/all_to_all | solution.py:101
  590.1 19.7 %copy-start.1 = (bf16[256,1024]{1,0:T(8,128)(2,1)S(1)}, bf16[256,1024]{1,0:T(8,128)(2,1)}, u32[]{:S(2)}) copy-start(bf16[256,1024]{1,0:T(8,128)(2,1)} %param.6) | copy-start | bytes 1572868
Sparse Core Ops, SparseCore 0:
  44.1 116.7 all-gather.2
  182.6 64.4 all-gather.4
where the time goes:
time: 617 us
  waiting for transfers between devices  427 us (69%)
  matrix products  73.4 us (12%)
  other arithmetic  48.8 us (8%)
  blocking collectives  38.6 us (6%)
  between operations  14.1 us (2%)
  starting transfers between devices  10.7 us (2%)
    ppermute x4, waiting for transfers between devices, swap_dp(): return lax.ppermute(value, 'dp', perm=[(0, 1), (1, 0)])  247 us
    all_gather x1, waiting for transfers between devices, local(): fragment = lax.all_gather(narrow_rows, 'tensor', axis=1, tiled=True)  115 us
    all_gather x1, waiting for transfers between devices, local(): other_rows = lax.all_gather(other_piece, 'tensor', axis=1, tiled=True)  64.6 us
    broadcast_in_dim x2, other arithmetic, local(): return (gate_grad[None], up_grad[None], down_grad[None], router_grad)  36.5 us
    all_to_all x1, blocking collectives, local(): lax.all_to_all(outgoing, 'expert', split_axis=0, concat_axis=0, tiled=True)  23.2 us
    dot_general x1, matrix products, local(): lax.dot_general(own_rows, local_weight, contract_cols, preferred_element_...  18.3 us
    dot_general x1, matrix products, local(): lax.dot_general(hidden, scaled_own, contract_rows, preferred_element_type...  18.3 us
    dot_general x1, matrix products, local(): lax.dot_general(other_rows, local_weight, contract_cols, preferred_elemen...  18.2 us
  transfers between devices with their start and end apart: 7, of which 4 were waited for; matrix products, arithmetic and copies ran while one was open for 12% of the time, Pallas kernels for 0%

commit v1 on v0

--- a/solution.py
+++ b/solution.py
@@ -2,6 +2,7 @@
 import jax.numpy as jnp
 from jax import lax
 from jax.sharding import PartitionSpec as P
+from jax.lax import axis_index, ppermute, psum
 
 PARTIAL_DTYPE = jnp.float32
 
@@ -65,7 +66,30 @@
         fragment, (1 - replica) * half + part * piece, piece, axis=1
     )
     other_piece = swap_dp(send_rows)
-    other_rows = lax.all_gather(other_piece, "tensor", axis=1, tiled=True)
+    r2, response, a_now = (psum(1, "tensor"), axis_index("tensor"), other_piece.shape[1])
+    in_order = []
+    for s, hop_no in enumerate(other_piece.shape):
+        in_order.append(hop_no * r2 if s == 1 else hop_no)
+    other_rows = lax.dynamic_update_slice_in_dim(
+        jnp.zeros(in_order, other_piece.dtype), other_piece, response * a_now, axis=1
+    )
+    z1 = even = other_piece
+    for to_i in [*range(1, r2 // 2 + 1)]:
+        made = []
+        for s in [*range(r2)]:
+            made.append((s, (s + 1) % r2))
+        z1 = ppermute(z1, "tensor", made)
+        other_rows = lax.dynamic_update_slice_in_dim(
+            other_rows, z1, (response - to_i) % r2 * a_now, axis=1
+        )
+        if 2 * to_i < r2:
+            all_blocks = []
+            for s in [*range(r2)]:
+                all_blocks.append((s, (s - 1) % r2))
+            even = ppermute(even, "tensor", all_blocks)
+            other_rows = lax.dynamic_update_slice_in_dim(
+                other_rows, even, (response + to_i) % r2 * a_now, axis=1
+            )
     hidden_other, other_rows = lax.optimization_barrier((hidden_other, other_rows))
     other_gates = swap_dp(gate_bf16).astype(jnp.float32)[:, None]
     local_weight = down_weight[0]

time: 617 us -> 603 us (0.977)
  waiting for transfers between devices: 427 us -> 406 us
    all_gather x1 -> x0, waiting for transfers between devices: 64.6 us -> none  [local(): other_rows = lax.all_gather(other_piece, 'tensor', axis=1, tiled=True)]
    ppermute x0 -> x3, waiting for transfers between devices: none -> 47.6 us  [the longest x2 32.6 us: local(): z1 = ppermute(z1, 'tensor', made)]
  transfers between devices with their start and end apart: 7 -> 9, of which waited for: 4 -> 6; matrix products, arithmetic and copies ran while one was open for 12% -> 13% of each run, Pallas kernels for 0% -> 0%
where the time goes in v1:
time: 603 us; the launch traced here: 602 us
  waiting for transfers between devices  406 us (67%)
  matrix products  72.7 us (12%)
  other arithmetic  48.8 us (8%)
  blocking collectives  39.1 us (6%)
  starting transfers between devices  16.5 us (3%)
  between operations  14.2 us (2%)
    ppermute x4, waiting for transfers between devices, swap_dp(): return lax.ppermute(value, 'dp', perm=[(0, 1), (1, 0)])  243 us
    all_gather x1, waiting for transfers between devices, local(): fragment = lax.all_gather(narrow_rows, 'tensor', axis=1, tiled=True)  115 us
    broadcast_in_dim x2, other arithmetic, local(): return (gate_grad[None], up_grad[None], down_grad[None], router_grad)  36.5 us
    ppermute x2, waiting for transfers between devices, local(): z1 = ppermute(z1, 'tensor', made)  32.6 us
    all_to_all x1, blocking collectives, local(): lax.all_to_all(outgoing, 'expert', split_axis=0, concat_axis=0, tiled=True)  23.2 us
    dot_general x1, matrix products, local(): lax.dot_general(other_rows, local_weight, contract_cols, preferred_elemen...  18.4 us
    dot_general x1, matrix products, local(): lax.dot_general(own_rows, local_weight, contract_cols, preferred_element_...  18.4 us
    dot_general x1, matrix products, local(): lax.dot_general(hidden, scaled_own, contract_rows, preferred_element_type...  18.3 us
  transfers between devices with their start and end apart: 9, of which 6 were waited for; matrix products, arithmetic and copies ran while one was open for 13% of the time, Pallas kernels for 0%

profile of v1, /device:TPU:1, one launch (start us, length us, event | category | flops | bytes accessed | tf_op | source)
XLA Modules:
  0.0 602.5 jit_solution(4797667077214926300)
XLA Ops:
  7.2 0.0 all-gather.2.cloned.1.call-start
  7.2 0.9 copy.28
  8.1 0.1 eq.63
  8.2 0.1 eq.59
  8.4 1.2 reduce-window.6
  9.6 0.2 slice_reduce_fusion
  9.8 0.2 reduce-window.9
  10.0 0.1 add_bitcast_fusion
  10.1 0.1 reduce_sum.48
  10.3 0.1 copy.30
  10.3 0.7 multiply_add_fusion
  11.1 8.8 %fusion.5 = bf16[768,3584]{1,0:T(8,128)(2,1)} fusion(bf16[1,768,3584]{2,1,0:T(8,128)(2,1)} %param.10, bf16[1,768,3584]{2,1,0:T(8,128)(2,1)} %param.9), kind=kLoop, calls=%fused_computation.13 | loop fusion | flops 22020096 | bytes 16515072 | tf_op jit(solution)/shard_map/convert_element_type | solution.py:45
  19.9 0.8 convolution_convert_fusion.2
  20.7 23.2 %all_to_all.20 = bf16[4,192,1024]{2,1,0:T(8,128)(2,1)} all-to-all(bf16[4,192,1024]{2,1,0:T(8,128)(2,1)S(1)} %bitcast.61), channel_id=1, replica_groups=mesh['dp'=2,'expert'=4,'tensor'=4] {'expert'}, dimensions={0} | all-to-all | bytes 3145728 | tf_op jit(solution)/shard_map/all_to_all | solution.py:54
  43.9 1.8 collective-permute-start
  45.7 115.1 %all-gather.2.cloned.1.call-done = bf16[768,4096]{1,0:T(8,128)(2,1)} async-done(((bf16[768,1024]{1,0:T(8,128)(2,1)}), bf16[768,4096]{1,0:T(8,128)(2,1)}) %all-gather.2.cloned.1.call-update) | async-done | bytes 6291472 | tf_op jit(solution)/shard_map/all_gather | solution.py:60
  160.8 1.2 constant_dynamic-slice_fusion
  162.0 1.2 collective-permute-start.1
  163.2 18.2 %collective-permute-done.1 = bf16[768,512]{1,0:T(8,128)(2,1)S(1)} collective-permute-done((bf16[768,512]{1,0:T(8,128)(2,1)S(1)}, bf16[768,512]{1,0:T(8,128)(2,1)S(1)}, u32[]{:S(2)}, u32[]{:S(2)}) %collective-permute-start.1) | collective-permute-done | bytes 786464 | tf_op jit(solution)/shard_map/ppermute | solution.py:16
  181.4 0.5 collective-permute-start.2
  182.0 2.8 collective-permute-start.3
  184.7 16.7 %collective-permute-done.2 = bf16[768,512]{1,0:T(8,128)(2,1)S(1)} collective-permute-done((bf16[768,512]{1,0:T(8,128)(2,1)S(1)}, bf16[768,512]{1,0:T(8,128)(2,1)S(1)}, u32[]{:S(2)}, u32[]{:S(2)}) %collective-permute-start.2) | collective-permute-done | bytes 786464 | tf_op jit(solution)/shard_map/ppermute | solution.py:81
  201.4 0.4 broadcast_in_dim.76
  201.8 0.1 constant_dynamic-update-slice_fusion.3
  201.9 0.1 constant_dynamic-update-slice_fusion.2
  202.0 14.9 %collective-permute-done.3 = bf16[768,512]{1,0:T(8,128)(2,1)} collective-permute-done((bf16[768,512]{1,0:T(8,128)(2,1)S(1)}, bf16[768,512]{1,0:T(8,128)(2,1)}, u32[]{:S(2)}, u32[]{:S(2)}) %collective-permute-start.3) | collective-permute-done | bytes 786464 | tf_op jit(solution)/shard_map/ppermute | solution.py:89
  217.0 1.2 constant_dynamic-update-slice_fusion.1
  218.2 15.9 %collective-permute-done.4 = bf16[768,512]{1,0:T(8,128)(2,1)S(1)} collective-permute-done((bf16[768,512]{1,0:T(8,128)(2,1)S(1)}, bf16[768,512]{1,0:T(8,128)(2,1)S(1)}, u32[]{:S(2)}, u32[]{:S(2)}) %collective-permute-start.4) | collective-permute-done | bytes 786464 | tf_op jit(solution)/shard_map/ppermute | solution.py:81
  234.1 0.1 constant_dynamic-update-slice_fusion
  234.3 18.4 %fusion.1 = f32[768,3584]{1,0:T(8,128)} fusion(bf16[768,2048]{1,0:T(8,128)(2,1)S(1)} %constant_dynamic-update-slice_fusion, bf16[1,3584,2048]{2,1,0:T(8,128)(2,1)} %param.11), kind=kOutput, calls=%fused_computation.7 | convolution fusion | flops 11274289152 | bytes 28835840 | tf_op jit(solution)/shard_map/dot_general | solution.py:96
  252.7 1.6 collective-permute-start.5
  254.3 0.2 select_reduce_fusion.2
  254.6 0.1 convert_element_type.113
  254.6 8.7 %all_to_all.21 = bf16[4,1,192]{2,1,0:T(2,128)(2,1)S(1)} all-to-all(bf16[4,1,192]{2,1,0:T(2,128)(2,1)S(1)} %convert_element_type.113), channel_id=1, replica_groups=mesh['dp'=2,'expert'=4,'tensor'=4] {'expert'}, dimensions={0} | all-to-all | bytes 3072 | tf_op jit(solution)/shard_map/all_to_all | solution.py:55
  263.3 0.1 reshape.71
  263.4 0.0 collective-permute-start.6
  263.5 225.2 %collective-permute-done.6 = bf16[768]{0:T(1024)(128)(2,1)S(1)} collective-permute-done((bf16[768]{0:T(1024)(128)(2,1)S(1)}, bf16[768]{0:T(1024)(128)(2,1)S(1)}, u32[]{:S(2)}, u32[]{:S(2)}) %collective-permute-start.6) | collective-permute-done | bytes 1568 | tf_op jit(solution)/shard_map/ppermute | solution.py:16
  488.7 18.3 %convolution_convert_fusion.1 = bf16[3584,2048]{1,0:T(8,128)(2,1)} fusion(bf16[768,3584]{1,0:T(8,128)(2,1)} %fusion.5, f32[768]{0:T(1024)S(1)} %convert_element_type.91, bf16[768,4096]{1,0:T(8,128)(2,1)} %all-gather.2.cloned.1.call-done, s32[]{:T(128)S(6)} %select_n.58), kind=kOutput, calls=%fused_computation.5 | convolution fusion | flops 11286347776 | bytes 23333892 | tf_op jit(solution)/shard_map/dot_general | solution.py:105
  507.0 18.4 %fusion.3 = f32[768,3584]{1,0:T(8,128)} fusion(bf16[1,3584,2048]{2,1,0:T(8,128)(2,1)} %param.11, bf16[768,4096]{1,0:T(8,128)(2,1)} %all-gather.2.cloned.1.call-done, s32[]{:T(128)S(6)} %select_n.58), kind=kOutput, calls=%fused_computation.9 | convolution fusion | flops 11274289152 | bytes 28835844 | tf_op jit(solution)/shard_map/dot_general | solution.py:100
  525.4 17.0 %convolution_convert_fusion = bf16[3584,2048]{1,0:T(8,128)(2,1)} fusion(bf16[768,3584]{1,0:T(8,128)(2,1)} %collective-permute-done, bf16[768,2048]{1,0:T(8,128)(2,1)S(1)} %copy-done.3, f32[768]{0:T(1024)S(1)} %convert_element_type.101), kind=kOutput, calls=%fused_computation.4 | convolution fusion | flops 11286347776 | bytes 23333888 | tf_op jit(solution)/shard_map/dot_general | solution.py:108
  542.3 17.8 %fusion.13 = (bf16[1,768,3584]{2,1,0:T(8,128)(2,1)}, bf16[1,768,3584]{2,1,0:T(8,128)(2,1)}, f32[768]{0:T(1024)S(1)}) fusion(f32[768]{0:T(1024)S(1)} %convert_element_type.91, bf16[1,768,3584]{2,1,0:T(8,128)(2,1)S(1)} %bitcast.59, f32[768,3584]{1,0:T(8,128)} %fusion.3, f32[768,3584]{1,0:T(8,128)} %collective-permute-done.5, bf16[1,768,3584]{2,1,0:T(8,128)(2,1)} %param.10, ...), kind=kLoop, calls=%fused_computation.25 | loop fusion | flops 55049472 | bytes 49551360 | tf_op jit(solution)/shard_map/broadcast_in_dim | solution.py:140
  560.2 0.1 all_to_all.15
  560.2 7.2 %psum.7 = f32[4,1,192]{2,1,0:T(1,128)} all-reduce(f32[4,1,192]{2,1,0:T(1,128)S(1)} %all_to_all.15), channel_id=1, replica_groups=mesh['dp'=2,'expert'=4,'tensor'=4] {'tensor'}, use_global_device_ids=true, to_apply=%region_5.6 | all-reduce | flops 768 | bytes 6144 | tf_op jit(solution)/shard_map/psum | solution.py:124
  567.4 8.5 %all-to-all-start.2 = ((f32[4,1,192]{2,1,0:T(1,128)}), f32[4,1,192]{2,1,0:T(1,128)S(1)}, u32[]{:S(2)}, u32[]{:S(2)}) async-start(f32[4,1,192]{2,1,0:T(1,128)} %psum.7), calls=%async_computation.2 | async-start | bytes 8192 | tf_op jit(solution)/shard_map/all_to_all | solution.py:125
  575.9 18.7 %fusion = bf16[1,3584,2048]{2,1,0:T(8,128)(2,1)} fusion(bf16[3584,2048]{1,0:T(8,128)(2,1)} %convolution_convert_fusion, bf16[3584,2048]{1,0:T(8,128)(2,1)} %convolution_convert_fusion.1), kind=kLoop, calls=%fused_computation.6 | loop fusion | flops 29360128 | bytes 44040192 | tf_op jit(solution)/shard_map/broadcast_in_dim | solution.py:140
  594.6 0.1 broadcast_in_dim.80
  594.7 0.3 select_reduce_fusion.1
  595.0 0.6 pad_maximum_fusion
  (28 shorter events, 0.2 us)
Async XLA Ops:
  7.2 12.7 %copy-start = (bf16[256,1024]{1,0:T(8,128)(2,1)S(1)}, bf16[256,1024]{1,0:T(8,128)(2,1)}, u32[]{:S(2)}) copy-start(bf16[256,1024]{1,0:T(8,128)(2,1)} %param.6) | copy-start | bytes 1572868
  7.2 153.6 %all-gather.2.cloned.1.call-start = ((), (), s32[]{:S(2)}) async-start(), calls=%async_computation.3 | async-start | bytes 7864320 | tf_op jit(solution)/shard_map/all_gather | solution.py:60
  43.9 190.3 %collective-permute-start = (bf16[768,3584]{1,0:T(8,128)(2,1)}, bf16[768,3584]{1,0:T(8,128)(2,1)}, u32[]{:S(2)}, u32[]{:S(2)}) collective-permute-start(bf16[768,3584]{1,0:T(8,128)(2,1)} %fusion.5), channel_id=1, source_target_pairs={{0,16},{16,0},{1,17},{17,1},{2,18},{18,2},{3,19},{19,3},{4,20},{20... | collective-permute-start | bytes 16515080 | tf_op jit(solution)/shard_map/ppermute | solution.py:16
  162.0 19.5 %collective-permute-start.1 = (bf16[768,512]{1,0:T(8,128)(2,1)S(1)}, bf16[768,512]{1,0:T(8,128)(2,1)S(1)}, u32[]{:S(2)}, u32[]{:S(2)}) collective-permute-start(bf16[768,512]{1,0:T(8,128)(2,1)S(1)} %constant_dynamic-slice_fusion), channel_id=1, source_target_pairs={{0,16},{16,0},{1,17},{17,1},{2,18},{18,2},{3,19},{19,3},{4,20},{20... | collective-permute-start | bytes 2359304 | tf_op jit(solution)/shard_map/ppermute | solution.py:16
  181.4 20.0 %collective-permute-start.2 = (bf16[768,512]{1,0:T(8,128)(2,1)S(1)}, bf16[768,512]{1,0:T(8,128)(2,1)S(1)}, u32[]{:S(2)}, u32[]{:S(2)}) collective-permute-start(bf16[768,512]{1,0:T(8,128)(2,1)S(1)} %collective-permute-done.1), channel_id=1, source_target_pairs={{0,1},{1,2},{2,3},{3,0},{4,5},{5,6},{6,7},{7,4},{8,9},{9,10},{10,1... | collective-permute-start | bytes 2359304 | tf_op jit(solution)/shard_map/ppermute | solution.py:81
  182.0 35.0 %collective-permute-start.3 = (bf16[768,512]{1,0:T(8,128)(2,1)S(1)}, bf16[768,512]{1,0:T(8,128)(2,1)}, u32[]{:S(2)}, u32[]{:S(2)}) collective-permute-start(bf16[768,512]{1,0:T(8,128)(2,1)S(1)} %collective-permute-done.1), channel_id=1, source_target_pairs={{0,3},{1,0},{2,1},{3,2},{4,7},{5,4},{6,5},{7,6},{8,11},{9,8},{10,9... | collective-permute-start | bytes 2359304 | tf_op jit(solution)/shard_map/ppermute | solution.py:89
  201.4 32.7 %collective-permute-start.4 = (bf16[768,512]{1,0:T(8,128)(2,1)S(1)}, bf16[768,512]{1,0:T(8,128)(2,1)S(1)}, u32[]{:S(2)}, u32[]{:S(2)}) collective-permute-start(bf16[768,512]{1,0:T(8,128)(2,1)S(1)} %collective-permute-done.2), channel_id=1, source_target_pairs={{0,1},{1,2},{2,3},{3,0},{4,5},{5,6},{6,7},{7,4},{8,9},{9,10},{10,1... | collective-permute-start | bytes 2359304 | tf_op jit(solution)/shard_map/ppermute | solution.py:81
  234.3 18.4 %copy-start.2 = (bf16[768,2048]{1,0:T(8,128)(2,1)}, bf16[768,2048]{1,0:T(8,128)(2,1)S(1)}, u32[]{:S(2)}) copy-start(bf16[768,2048]{1,0:T(8,128)(2,1)S(1)} %constant_dynamic-update-slice_fusion) | copy-start | bytes 9437188
  234.3 20.1 %copy-start.4 = (bf16[256,2]{0,1:T(2,128)(2,1)S(1)}, bf16[256,2]{0,1:T(2,128)(2,1)}, u32[]{:S(2)}) copy-start(bf16[256,2]{0,1:T(2,128)(2,1)} %param.8) | copy-start | bytes 3076
  252.7 289.6 %collective-permute-start.5 = (f32[768,3584]{1,0:T(8,128)}, f32[768,3584]{1,0:T(8,128)}, u32[]{:S(2)}, u32[]{:S(2)}) collective-permute-start(f32[768,3584]{1,0:T(8,128)} %fusion.1), channel_id=1, source_target_pairs={{0,16},{16,0},{1,17},{17,1},{2,18},{18,2},{3,19},{19,3},{4,20},{20... | collective-permute-start | bytes 33030152 | tf_op jit(solution)/shard_map/ppermute | solution.py:16
  263.4 225.3 %collective-permute-start.6 = (bf16[768]{0:T(1024)(128)(2,1)S(1)}, bf16[768]{0:T(1024)(128)(2,1)S(1)}, u32[]{:S(2)}, u32[]{:S(2)}) collective-permute-start(bf16[768]{0:T(1024)(128)(2,1)S(1)} %reshape.71), channel_id=1, source_target_pairs={{0,16},{16,0},{1,17},{17,1},{2,18},{18,2},{3,19},{19,3},{4,20},{20... | collective-permute-start | bytes 4616 | tf_op jit(solution)/shard_map/ppermute | solution.py:16
  488.7 53.6 %slice-start = ((s8[5505024]{0:T(1024)(128)(4,1)}), s8[4194304]{0:T(1024)(128)(4,1)S(1)}, s32[]{:S(2)}) async-start(s8[5505024]{0:T(1024)(128)(4,1)} %bitcast.58), calls=%async_computation.4 | async-start | bytes 8388608
  507.0 18.4 %copy-start.3 = (bf16[768,2048]{1,0:T(8,128)(2,1)S(1)}, bf16[768,2048]{1,0:T(8,128)(2,1)}, u32[]{:S(2)}) copy-start(bf16[768,2048]{1,0:T(8,128)(2,1)} %copy-done.2) | copy-start | bytes 9437188
  507.0 35.3 %slice-start.1 = ((s8[5505024]{0:T(1024)(128)(4,1)}), s8[1310720]{0:T(1024)(128)(4,1)S(1)}, s32[]{:S(2)}) async-start(s8[5505024]{0:T(1024)(128)(4,1)} %bitcast.58), calls=%async_computation.5 | async-start | bytes 2621440
  567.4 27.1 %all-to-all-start.2 = ((f32[4,1,192]{2,1,0:T(1,128)}), f32[4,1,192]{2,1,0:T(1,128)S(1)}, u32[]{:S(2)}, u32[]{:S(2)}) async-start(f32[4,1,192]{2,1,0:T(1,128)} %psum.7), calls=%async_computation.2 | async-start | bytes 8192 | tf_op jit(solution)/shard_map/all_to_all | solution.py:125
  575.9 19.7 %copy-start.1 = (bf16[256,1024]{1,0:T(8,128)(2,1)S(1)}, bf16[256,1024]{1,0:T(8,128)(2,1)}, u32[]{:S(2)}) copy-start(bf16[256,1024]{1,0:T(8,128)(2,1)} %param.6) | copy-start | bytes 1572868
Sparse Core Ops, SparseCore 0:
  44.1 116.7 all-gather.1
